TPU v7x, 32 devices: a whole 2x2x4 slice. The times are simulated.
32 devices in a mesh: tok: 2 (over x), voc: 4 (over y, core), wid: 4 (over z).
Axes of the slice: x: 2, y: 2, z: 4, core: 2. Of those that a mesh axis runs over, the one named last changes fastest.
Arguments:
- hidden: bfloat16 [512, 8192], P('tok', 'wid'), may hold values from -1500 to 1500
- proj: bfloat16 [3584, 8192], P('voc', 'wid'), may hold values from -0.0625 to 0.0625
- table: bfloat16 [19456, 3584], P(('voc', 'wid'), 'tok'), may hold values from -10 to 10
- targets: int32 [512], P('tok'), may hold values from 0 to 19455
- valid: int32 [512], P('tok'), may hold values from 0 to 1, as said below
Outputs:
- grad_proj: float32 [3584, 8192], P('voc', 'wid')
- loss: float32 [], replicated
Inputs may be any that keep to these rules, and one draw needn't show every extreme that they name: `valid`: position 0 is always scored.
All inputs are finite; a program needn't handle non-finite values.
Results may differ from a plain program's by a relative error of at most 0.008.
Values may be sent and summed in bfloat16 or wider, within the bound.
No kernel may reach another device: no remote copies, remote signals or barrier semaphores. Data moves between devices by JAX's collectives and lax.ppermute only.
A program may use at most 128 MiB of HBM per device.

v0:
```python
import jax
import jax.numpy as jnp
from jax import lax
from jax.sharding import PartitionSpec as P


def on_device(hidden, proj, table, targets, valid):
    tok_rows = hidden.shape[0]
    block_rows = table.shape[0]
    partial_value = lax.dot_general(
        hidden, proj, (((1,), (1,)), ((), ())), preferred_element_type=jnp.float32
    )
    summed = lax.psum(partial_value, "wid")
    projected = lax.all_gather(summed.astype(jnp.bfloat16), "voc", axis=1, tiled=True)
    full_table = lax.all_gather(table, "tok", axis=1, tiled=True)
    logits = lax.dot_general(
        projected, full_table, (((1,), (1,)), ((), ())), preferred_element_type=jnp.float32
    )
    block_base = (lax.axis_index("voc") * lax.axis_size("wid") + lax.axis_index("wid")) * block_rows
    local_ids = targets - block_base
    is_target = local_ids[:, None] == lax.broadcasted_iota(jnp.int32, (tok_rows, block_rows), 1)
    picked_here = jnp.sum(jnp.where(is_target, logits, 0.0), axis=1)
    peak_here = jnp.max(logits, axis=1)
    row_peak = lax.pmax(peak_here, ("voc", "wid"))
    exp_here = jnp.sum(jnp.exp(logits - row_peak[:, None]), axis=1)
    row_total, picked = lax.psum((exp_here, picked_here), ("voc", "wid"))
    log_total = row_peak + jnp.log(row_total)
    weight = valid.astype(jnp.float32)
    dlogits = (
        weight[:, None] * (jnp.exp(logits - log_total[:, None]) - is_target.astype(jnp.float32))
    ).astype(jnp.bfloat16)
    reduced = lax.psum_scatter(
        lax.dot_general(
            full_table, dlogits, (((0,), (1,)), ((), ())), preferred_element_type=jnp.float32
        ),
        "voc",
        scatter_dimension=0,
        tiled=True,
    )
    grad_rows = lax.psum(reduced, "wid").astype(jnp.bfloat16)
    grad_part = jnp.dot(grad_rows, hidden, preferred_element_type=jnp.float32)
    loss_part = jnp.sum(weight * (log_total - picked))
    count_part = jnp.sum(weight)
    grad_proj, loss_sum, position_count = lax.psum((grad_part, loss_part, count_part), "tok")
    return (grad_proj, loss_sum / position_count)


def solution(mesh):
    return jax.shard_map(
        on_device,
        mesh=mesh,
        in_specs=(P("tok", "wid"), P("voc", "wid"), P(("voc", "wid"), "tok"), P("tok"), P("tok")),
        out_specs=(P("voc", "wid"), P()),
        check_vma=False,
    )
```

profile of v0, /device:TPU:0, one launch (start us, length us, event | category | flops | bytes accessed | tf_op | source)
XLA Modules:
  0.0 535.9 jit_solution(15466897181801371139)
XLA Ops:
  7.2 0.0 copy-start
  7.2 0.0 all-gather.3.cloned.1.call-start
  7.2 1.2 copy-done
  8.4 3.3 fusion.6
  11.7 41.0 %all-reduce.7 = bf16[256,896]{1,0:T(8,128)(2,1)} all-reduce(f32[256,896]{1,0:T(8,128)S(1)} %fusion.6), channel_id=1, replica_groups=mesh['tok'=2,'voc'=4,'wid'=4] {'wid'}, use_global_device_ids=true, to_apply=%region_0.0 | all-reduce | flops 229376 | bytes 1376256 | tf_op jit(solution)/shard_map/psum | solution.py:13
  52.7 0.0 all-gather.3.cloned.1.call-update
  52.7 0.0 copy-start.1
  52.7 0.0 copy-start.2
  52.7 0.0 all-gather.5.cloned.1.call-start
  52.8 0.7 all-gather.5.cloned.1.call-update
  53.5 0.0 reduce-scatter.2.cloned.1.call-start
  53.5 0.0 copy-done.1
  53.6 0.0 copy-done.2
  53.6 19.9 %all-gather.3.cloned.1.call-done = bf16[256,3584]{1,0:T(8,128)(2,1)} async-done(((bf16[256,896]{1,0:T(8,128)(2,1)}), bf16[256,3584]{1,0:T(8,128)(2,1)}) %all-gather.3.cloned.1.call-update) | async-done | bytes 1835024 | tf_op jit(solution)/shard_map/all_gather | solution.py:14
  73.5 111.7 %all-gather.5.cloned.1.call-done = bf16[1216,3584]{1,0:T(8,128)(2,1)} async-done(((bf16[1216,1792]{1,0:T(8,128)(2,1)}), bf16[1216,3584]{1,0:T(8,128)(2,1)}) %all-gather.5.cloned.1.call-update) | async-done | bytes 8716304 | tf_op jit(solution)/shard_map/all_gather | solution.py:15
  185.1 6.5 %fusion.5 = (f32[256]{0:T(256)S(1)}, f32[256,1216]{0,1:T(8,128)S(1)}) fusion(bf16[256,3584]{1,0:T(8,128)(2,1)} %all-gather.3.cloned.1.call-done, bf16[1216,3584]{1,0:T(8,128)(2,1)} %all-gather.5.cloned.1.call-done), kind=kOutput, calls=%fused_computation.14 | convolution fusion | flops 2231680768 | bytes 11797504 | tf_op jit(solution)/shard_map/dot_general | solution.py:16
  191.6 33.4 %pmax.7 = f32[256]{0:T(256)S(1)} all-reduce(f32[256]{0:T(256)S(1)} %get-tuple-element.11), channel_id=1, replica_groups=mesh['tok'=2,'voc'=4,'wid'=4] {'voc','wid'}, use_global_device_ids=true, to_apply=%region_2.3 | all-reduce | flops 256 | bytes 2048 | tf_op jit(solution)/shard_map/pmax | solution.py:24
  225.0 0.3 select_reduce_fusion
  225.4 29.7 %all-reduce = (f32[256]{0:T(256)S(1)}, f32[256]{0:T(256)S(1)}) all-reduce(f32[256]{0:T(256)S(1)} %get-tuple-element.3, f32[256]{0:T(256)S(1)} %get-tuple-element.2), channel_id=1, replica_groups=mesh['tok'=2,'voc'=4,'wid'=4] {'voc','wid'}, use_global_device_ids=true, to_apply=%region_4.5 | all-reduce | flops 512 | bytes 4096 | tf_op jit(solution)/shard_map/psum | solution.py:26
  255.0 0.6 convert_reduce_fusion
  255.7 7.9 %convolution_bitcast_fusion = f32[3584,256]{0,1:T(8,128)} fusion(bf16[1216,3584]{1,0:T(8,128)(2,1)} %all-gather.5.cloned.1.call-done, f32[256,1216]{0,1:T(8,128)S(1)} %get-tuple-element.12, s32[256]{0:T(256)S(1)} %broadcast_subtract_fusion, f32[256]{0:T(256)S(1)} %get-tuple-element.10, f32[256]{0:T(256)S(1)} %convert_element_type.15), kind=kOutput, calls=%fused_computation | convolution fusion | flops 2233237504 | bytes 13634560 | tf_op jit(solution)/shard_map/dot_general | solution.py:33
  263.6 0.0 reduce-scatter.2.cloned.1.call-update
  263.6 0.0 all-reduce.6.cloned.1.call-start
  263.7 39.4 %reduce-scatter.2.cloned.1.call-done = f32[896,256]{0,1:T(8,128)} async-done(((f32[3584,256]{0,1:T(8,128)}), f32[896,256]{0,1:T(8,128)}) %reduce-scatter.2.cloned.1.call-update) | async-done | bytes 917520 | tf_op jit(solution)/shard_map/reduce_scatter | solution.py:32
  303.1 39.8 %all-reduce.8 = bf16[896,256]{0,1:T(8,128)(2,1)S(1)} all-reduce(f32[896,256]{0,1:T(8,128)} %reduce-scatter.2.cloned.1.call-done), channel_id=1, replica_groups=mesh['tok'=2,'voc'=4,'wid'=4] {'wid'}, use_global_device_ids=true, to_apply=%region_6.7 | all-reduce | flops 229376 | bytes 1376256 | tf_op jit(solution)/shard_map/psum | solution.py:40
  342.9 4.2 fusion.7
  347.1 0.0 all-reduce.6.cloned.1.call-update
  347.1 5.7 %all-reduce.1 = (f32[]{:T(128)}, f32[]{:T(128)}) all-reduce(f32[]{:T(128)} %get-tuple-element.5, f32[]{:T(128)} %get-tuple-element.4), channel_id=1, replica_groups=mesh['tok'=2,'voc'=4,'wid'=4] {'tok'}, use_global_device_ids=true, to_apply=%region_11.12 | all-reduce | flops 2 | bytes 16 | tf_op jit(solution)/shard_map/psum | solution.py:44
  354.2 167.0 %all-reduce.6.cloned.1.call-done = f32[896,2048]{1,0:T(8,128)} async-done(((f32[896,2048]{1,0:T(8,128)}), f32[896,2048]{1,0:T(8,128)}) %all-reduce.6.cloned.1.call-update) | async-done | bytes 7340048 | tf_op jit(solution)/shard_map/psum | solution.py:44
  521.2 7.1 %copy.12 = f32[896,2048]{1,0:T(8,128)} copy(f32[896,2048]{1,0:T(8,128)} %all-reduce.6.cloned.1.call-done) | data formatting | bytes 14680064
  (2 shorter events, 0.0 us)
Async XLA Ops:
  7.2 1.2 copy-start
  7.2 66.3 %all-gather.3.cloned.1.call-start = ((), (), s32[]{:S(2)}) async-start(), calls=%async_computation.1 | async-start | bytes 2293760 | tf_op jit(solution)/shard_map/all_gather | solution.py:14
  52.7 0.8 copy-start.1
  52.7 0.8 copy-start.2
  52.7 132.4 %all-gather.5.cloned.1.call-start = ((), (), s32[]{:S(2)}) async-start(), calls=%async_computation.2 | async-start | bytes 13074432 | tf_op jit(solution)/shard_map/all_gather | solution.py:15
  53.5 249.6 %reduce-scatter.2.cloned.1.call-start = ((), (), s32[]{:S(2)}) async-start(), calls=%async_computation.3 | async-start | bytes 4587520 | tf_op jit(solution)/shard_map/reduce_scatter | solution.py:32
  263.6 257.6 %all-reduce.6.cloned.1.call-start = ((), (), s32[]{:S(2)}) async-start(), calls=%async_computation.4 | async-start | bytes 14680064 | tf_op jit(solution)/shard_map/psum | solution.py:44
Sparse Core Ops, SparseCore 0:
  52.8 20.5 all-gather.2
  75.0 110.0 all-gather.4
  263.7 39.2 reduce-scatter.1
  347.3 173.8 all-reduce.5
where the time goes:
time: 536 us
  waiting for transfers between devices  339 us (63%)
  blocking collectives  150 us (28%)
  matrix products  21.9 us (4%)
  between operations  16.4 us (3%)
  local copies, waits for them, and re-layouts  8.27 us (2%)
    psum x1, waiting for transfers between devices, on_device(): lax.psum((grad_part, loss_part, count_part), 'tok')  167 us
    all_gather x1, waiting for transfers between devices, on_device(): full_table = lax.all_gather(table, 'tok', axis=1, tiled=True)  112 us
    psum x1, blocking collectives, on_device(): summed = lax.psum(partial_value, 'wid')  41 us
    psum x1, blocking collectives, on_device(): grad_rows = lax.psum(reduced, 'wid').astype(jnp.bfloat16)  39.8 us
    reduce_scatter x1, waiting for transfers between devices, on_device(): lax.psum_scatter(lax.dot_general(full_table, dlogits, (((0,), (1,)), ((),...  39.4 us
    pmax x1, blocking collectives, on_device(): row_peak = lax.pmax(peak_here, ('voc', 'wid'))  33.4 us
    psum x1, blocking collectives, on_device(): row_total, picked = lax.psum((exp_here, picked_here), ('voc', 'wid'))  29.7 us
    all_gather x1, waiting for transfers between devices, on_device(): lax.all_gather(summed.astype(jnp.bfloat16), 'voc', axis=1, tiled=True)  19.9 us
  transfers between devices with their start and end apart: 4, of which 4 were waited for; matrix products, arithmetic and copies ran while one was open for 0% of the time, Pallas kernels for 0%

commit v1 on v0

--- a/solution.py
+++ b/solution.py
@@ -10,7 +10,7 @@
     partial_value = lax.dot_general(
         hidden, proj, (((1,), (1,)), ((), ())), preferred_element_type=jnp.float32
     )
-    summed = lax.psum(partial_value, "wid")
+    summed = jnp.sum(lax.all_gather(partial_value, "wid"), axis=0)
     projected = lax.all_gather(summed.astype(jnp.bfloat16), "voc", axis=1, tiled=True)
     full_table = lax.all_gather(table, "tok", axis=1, tiled=True)
     logits = lax.dot_general(

time: 536 us -> 574 us (1.071)
  waiting for transfers between devices: 339 us -> 413 us
  blocking collectives: 150 us -> 109 us
    all_gather x0 -> x1, waiting for transfers between devices: none -> 74.9 us  [on_device(): summed = jnp.sum(lax.all_gather(partial_value, 'wid'), axis=0)]
    psum x1 -> x0, blocking collectives: 41 us -> none  [on_device(): summed = lax.psum(partial_value, 'wid')]
  transfers between devices with their start and end apart: 4 -> 5, of which waited for: 4 -> 5; matrix products, arithmetic and copies ran while one was open for 0% -> 0% of each run, Pallas kernels for 0% -> 0%
where the time goes in v1:
time: 574 us; the launch traced here: 573 us
  waiting for transfers between devices  413 us (72%)
  blocking collectives  109 us (19%)
  matrix products  22.9 us (4%)
  between operations  16.4 us (3%)
  local copies, waits for them, and re-layouts  8.27 us (1%)
    psum x1, waiting for transfers between devices, on_device(): lax.psum((grad_part, loss_part, count_part), 'tok')  167 us
    all_gather x1, waiting for transfers between devices, on_device(): full_table = lax.all_gather(table, 'tok', axis=1, tiled=True)  112 us
    all_gather x1, waiting for transfers between devices, on_device(): summed = jnp.sum(lax.all_gather(partial_value, 'wid'), axis=0)  74.9 us
    psum x1, blocking collectives, on_device(): grad_rows = lax.psum(reduced, 'wid').astype(jnp.bfloat16)  39.9 us
    reduce_scatter x1, waiting for transfers between devices, on_device(): lax.psum_scatter(lax.dot_general(full_table, dlogits, (((0,), (1,)), ((),...  39.4 us
    pmax x1, blocking collectives, on_device(): row_peak = lax.pmax(peak_here, ('voc', 'wid'))  33.4 us
    psum x1, blocking collectives, on_device(): row_total, picked = lax.psum((exp_here, picked_here), ('voc', 'wid'))  29.7 us
    all_gather x1, waiting for transfers between devices, on_device(): lax.all_gather(summed.astype(jnp.bfloat16), 'voc', axis=1, tiled=True)  19 us
  transfers between devices with their start and end apart: 5, of which 5 were waited for; matrix products, arithmetic and copies ran while one was open for 0% of the time, Pallas kernels for 0%

profile of v1, /device:TPU:0, one launch (start us, length us, event | category | flops | bytes accessed | tf_op | source)
XLA Modules:
  0.0 573.2 jit_solution(4906249613210148052)
XLA Ops:
  7.2 0.0 copy-start
  7.2 0.0 all-gather.9.cloned.1.call-start
  7.2 1.2 copy-done
  8.4 4.2 fusion.6
  12.6 0.0 all-gather.9.cloned.1.call-update
  12.7 0.0 all-gather.5.cloned.1.call-start
  12.7 74.9 %all-gather.9.cloned.1.call-done = f32[1024,896]{1,0:T(8,128)} async-done(((f32[256,896]{1,0:T(8,128)}), f32[1024,896]{1,0:T(8,128)}) %all-gather.9.cloned.1.call-update) | async-done | bytes 3670032 | tf_op jit(solution)/shard_map/all_gather | solution.py:13
  87.6 3.1 reduce_sum.45
  90.8 0.0 all-gather.5.cloned.1.call-update
  90.8 0.0 copy-start.1
  90.8 0.0 copy-start.2
  90.8 0.0 all-gather.7.cloned.1.call-start
  90.9 0.7 all-gather.7.cloned.1.call-update
  91.6 0.0 reduce-scatter.2.cloned.1.call-start
  91.6 0.0 copy-done.1
  91.7 19.0 %all-gather.5.cloned.1.call-done = bf16[256,3584]{1,0:T(8,128)(2,1)} async-done(((bf16[256,896]{1,0:T(8,128)(2,1)}), bf16[256,3584]{1,0:T(8,128)(2,1)}) %all-gather.5.cloned.1.call-update) | async-done | bytes 1835024 | tf_op jit(solution)/shard_map/all_gather | solution.py:14
  110.7 111.7 %all-gather.7.cloned.1.call-done = bf16[1216,3584]{1,0:T(8,128)(2,1)} async-done(((bf16[1216,1792]{1,0:T(8,128)(2,1)}), bf16[1216,3584]{1,0:T(8,128)(2,1)}) %all-gather.7.cloned.1.call-update) | async-done | bytes 8716304 | tf_op jit(solution)/shard_map/all_gather | solution.py:15
  222.4 6.5 %fusion.5 = (f32[256]{0:T(256)S(1)}, f32[256,1216]{0,1:T(8,128)S(1)}) fusion(bf16[256,3584]{1,0:T(8,128)(2,1)} %all-gather.5.cloned.1.call-done, bf16[1216,3584]{1,0:T(8,128)(2,1)} %all-gather.7.cloned.1.call-done), kind=kOutput, calls=%fused_computation.14 | convolution fusion | flops 2231680768 | bytes 11797504 | tf_op jit(solution)/shard_map/dot_general | solution.py:16
  228.9 33.4 %pmax.7 = f32[256]{0:T(256)S(1)} all-reduce(f32[256]{0:T(256)S(1)} %get-tuple-element.11), channel_id=1, replica_groups=mesh['tok'=2,'voc'=4,'wid'=4] {'voc','wid'}, use_global_device_ids=true, to_apply=%region_2.3 | all-reduce | flops 256 | bytes 2048 | tf_op jit(solution)/shard_map/pmax | solution.py:24
  262.3 0.3 select_reduce_fusion
  262.6 29.7 %all-reduce = (f32[256]{0:T(256)S(1)}, f32[256]{0:T(256)S(1)}) all-reduce(f32[256]{0:T(256)S(1)} %get-tuple-element.3, f32[256]{0:T(256)S(1)} %get-tuple-element.2), channel_id=1, replica_groups=mesh['tok'=2,'voc'=4,'wid'=4] {'voc','wid'}, use_global_device_ids=true, to_apply=%region_4.5 | all-reduce | flops 512 | bytes 4096 | tf_op jit(solution)/shard_map/psum | solution.py:26
  292.3 0.6 convert_reduce_fusion
  292.9 7.9 %convolution_bitcast_fusion = f32[3584,256]{0,1:T(8,128)} fusion(bf16[1216,3584]{1,0:T(8,128)(2,1)} %all-gather.7.cloned.1.call-done, f32[256,1216]{0,1:T(8,128)S(1)} %get-tuple-element.12, s32[256]{0:T(256)S(1)} %broadcast_subtract_fusion, f32[256]{0:T(256)S(1)} %get-tuple-element.10, f32[256]{0:T(256)S(1)} %convert_element_type.15), kind=kOutput, calls=%fused_computation | convolution fusion | flops 2233237504 | bytes 13634560 | tf_op jit(solution)/shard_map/dot_general | solution.py:33
  300.8 0.0 reduce-scatter.2.cloned.1.call-update
  300.9 0.0 all-reduce.5.cloned.1.call-start
  300.9 39.4 %reduce-scatter.2.cloned.1.call-done = f32[896,256]{0,1:T(8,128)} async-done(((f32[3584,256]{0,1:T(8,128)}), f32[896,256]{0,1:T(8,128)}) %reduce-scatter.2.cloned.1.call-update) | async-done | bytes 917520 | tf_op jit(solution)/shard_map/reduce_scatter | solution.py:32
  340.3 39.9 %all-reduce.6 = bf16[896,256]{0,1:T(8,128)(2,1)S(1)} all-reduce(f32[896,256]{0,1:T(8,128)} %reduce-scatter.2.cloned.1.call-done), channel_id=1, replica_groups=mesh['tok'=2,'voc'=4,'wid'=4] {'wid'}, use_global_device_ids=true, to_apply=%region_6.7 | all-reduce | flops 229376 | bytes 1376256 | tf_op jit(solution)/shard_map/psum | solution.py:40
  380.2 4.2 fusion.7
  384.4 0.0 all-reduce.5.cloned.1.call-update
  384.4 5.7 all-reduce.1
  391.4 167.0 %all-reduce.5.cloned.1.call-done = f32[896,2048]{1,0:T(8,128)} async-done(((f32[896,2048]{1,0:T(8,128)}), f32[896,2048]{1,0:T(8,128)}) %all-reduce.5.cloned.1.call-update) | async-done | bytes 7340048 | tf_op jit(solution)/shard_map/psum | solution.py:44
  558.4 7.1 %copy.10 = f32[896,2048]{1,0:T(8,128)} copy(f32[896,2048]{1,0:T(8,128)} %all-reduce.5.cloned.1.call-done) | data formatting | bytes 14680064
  (3 shorter events, 0.0 us)
Async XLA Ops:
  7.2 1.2 copy-start
  7.2 80.4 %all-gather.9.cloned.1.call-start = ((), (), s32[]{:S(2)}) async-start(), calls=%async_computation.5 | async-start | bytes 4587520 | tf_op jit(solution)/shard_map/all_gather | solution.py:13
  12.7 98.0 %all-gather.5.cloned.1.call-start = ((), (), s32[]{:S(2)}) async-start(), calls=%async_computation.1 | async-start | bytes 2293760 | tf_op jit(solution)/shard_map/all_gather | solution.py:14
  90.8 0.8 copy-start.1
  90.8 0.8 copy-start.2
  90.8 131.5 %all-gather.7.cloned.1.call-start = ((), (), s32[]{:S(2)}) async-start(), calls=%async_computation.2 | async-start | bytes 13074432 | tf_op jit(solution)/shard_map/all_gather | solution.py:15
  91.6 248.7 %reduce-scatter.2.cloned.1.call-start = ((), (), s32[]{:S(2)}) async-start(), calls=%async_computation.3 | async-start | bytes 4587520 | tf_op jit(solution)/shard_map/reduce_scatter | solution.py:32
  300.9 257.6 %all-reduce.5.cloned.1.call-start = ((), (), s32[]{:S(2)}) async-start(), calls=%async_computation.4 | async-start | bytes 14680064 | tf_op jit(solution)/shard_map/psum | solution.py:44
Sparse Core Ops, SparseCore 0:
  12.8 74.7 all-gather.8
  90.9 19.7 all-gather.4
  112.2 110.0 all-gather.6
  301.0 39.2 reduce-scatter.1
  384.5 173.8 all-reduce.4
